TPU v7x, 32 devices: a whole 2x2x4 slice. The times are simulated.
32 devices in a mesh: dp: 16 (over z, x, core), tm: 2 (over y).
Axes of the slice: x: 2, y: 2, z: 4, core: 2. Of those that a mesh axis runs over, the one named last changes fastest.
Arguments:
- src_mel: bfloat16 [2, 128, 640], P('tm', 'dp'), may hold values from -6 to 6
- owner: int32 [2, 128], P('tm', 'dp'), may hold values from 0 to 15, as said below
- dst_pos: int32 [2, 128], P('tm', 'dp'), may hold values from 0 to 7, as said below
- keep: int32 [2, 128], P('tm', 'dp'), may hold values 0 or 1
- cotangent: bfloat16 [16, 1024, 256], P('dp', 'tm'), may hold values from -0.125 to 0.125
- w_pre: bfloat16 [560, 512], replicated, may hold values from -0.25 to 0.25
- b_pre: float32 [512], replicated, may hold values from -3 to 3
- w_ups: bfloat16 [512, 4096], P('tm'), may hold values from -0.1875 to 0.1875
- upsample_bias: float32 [256], replicated, may hold values from -3 to 3
- w_res: bfloat16 [768, 256], replicated, may hold values from -0.21875 to 0.21875
- b_res: float32 [256], replicated, may hold values from -3 to 3
Outputs:
- section_out: bfloat16 [16, 1024, 256], P('dp', 'tm')
- grad_w_pre: float32 [560, 512], replicated
- grad_b_pre: float32 [512], replicated
- grad_w_res: float32 [768, 256], replicated
- grad_b_res: float32 [256], replicated
Inputs may be any that keep to these rules, and one draw needn't show every extreme that they name: Within one tm column, every dp index sends at most one of its segments to each owner, and every owner receives exactly 8 segments. `dst_pos`: the segments received by one owner in one column have positions 0 to 7, each once.
All inputs are finite; a program needn't handle non-finite values. No bound on the sum of `keep` on one device may be relied on, other than what follows from the above.
Results may differ from a plain program's by a relative error of at most 0.009.
The roundings to bfloat16 on the way count: a program that leaves them out, or rounds other values in their place, can miss the bound.
Values may be sent and summed in bfloat16 or wider, within the bound.
No kernel may reach another device: no remote copies, remote signals or barrier semaphores. Data moves between devices by JAX's collectives and lax.ppermute only.
A program may use at most 64 MiB of HBM per device.

v0:
```python
import jax
import jax.numpy as jnp
from jax import lax
from jax.sharding import PartitionSpec as P

KPRE = 7
UPSAMPLE_FACTOR = 8
DILATION_SIZE = 3


def with_halo(block, sides, width):
    for axis, dim in sides:
        count = lax.axis_size(axis)
        forward = [(i, i + 1) for i in range(count - 1)]
        backward = [(target, source) for source, target in forward]
        low = lax.ppermute(
            lax.slice_in_dim(block, block.shape[dim] - width, None, axis=dim), axis, forward
        )
        high = lax.ppermute(lax.slice_in_dim(block, 0, width, axis=dim), axis, backward)
        block = jnp.concatenate([low, block, high], axis=dim)
    return block


def leaky(value):
    return jnp.where(value > 0, value, 0.1 * value)


def negative_slope(value):
    return jnp.where(value > 0, 1.0, 0.1).astype(jnp.float32)


def contract_rows(left, right):
    return lax.dot_general(
        left, right, (((0,), (0,)), ((), ())), preferred_element_type=jnp.float32
    )


def contract_cols(left, right):
    return lax.dot_general(
        left, right, (((1,), (1,)), ((), ())), preferred_element_type=jnp.float32
    )


def local_pass(
    mel_ext,
    gradient_value,
    first_frame0,
    total,
    w_pre,
    b_pre,
    ups_forward,
    ups_backward,
    upsample_bias,
    w_res,
    b_res,
):
    mel_bins = mel_ext.shape[1]
    kpre = w_pre.shape[0] // mel_bins
    edge = kpre // 2 + 1
    frame_count = mel_ext.shape[0] - 2 * edge
    window_width = upsample_bias.shape[0]
    residual_kernel = w_res.shape[0] // window_width
    patches = jnp.concatenate([mel_ext[i : i + frame_count + 2] for i in range(kpre)], axis=1)
    pre = jnp.dot(patches, w_pre, preferred_element_type=jnp.float32) + b_pre
    frame_idx = first_frame0 - 1 + jnp.arange(frame_count + 2, dtype=jnp.int32)
    inside_f = ((frame_idx >= 0) & (frame_idx < total))[:, None]
    act = jnp.where(inside_f, leaky(pre), 0.0).astype(jnp.bfloat16)
    taps = ups_forward(act).reshape(frame_count + 2, 2 * UPSAMPLE_FACTOR, window_width)
    upper_output = taps[1:, :UPSAMPLE_FACTOR] + taps[:-1, UPSAMPLE_FACTOR:]
    sample_count = UPSAMPLE_FACTOR * frame_count
    start_offset = UPSAMPLE_FACTOR // 2 - DILATION_SIZE
    waveform = (
        upper_output.reshape(UPSAMPLE_FACTOR * (frame_count + 1), window_width)[
            start_offset : start_offset + sample_count + 2 * DILATION_SIZE
        ]
        + upsample_bias
    )
    step_index = (
        UPSAMPLE_FACTOR * first_frame0
        - DILATION_SIZE
        + jnp.arange(sample_count + 2 * DILATION_SIZE, dtype=jnp.int32)
    )
    inside_samples = ((step_index >= 0) & (step_index < UPSAMPLE_FACTOR * total))[:, None]
    hidden_state = jnp.where(inside_samples, leaky(waveform), 0.0).astype(jnp.bfloat16)
    column_block = jnp.concatenate(
        [
            hidden_state[kernel_index * DILATION_SIZE : kernel_index * DILATION_SIZE + sample_count]
            for kernel_index in range(residual_kernel)
        ],
        axis=1,
    )
    convolve_fn = jnp.dot(column_block, w_res, preferred_element_type=jnp.float32) + b_res
    output_rows = (waveform[DILATION_SIZE : DILATION_SIZE + sample_count] + convolve_fn).astype(
        jnp.bfloat16
    )
    g_wres = contract_rows(column_block, gradient_value)
    g_bres = jnp.sum(gradient_value.astype(jnp.float32), axis=0)
    backward_pass = contract_cols(gradient_value, w_res)
    hidden_gradient = jnp.zeros((sample_count + 2 * DILATION_SIZE, window_width), jnp.float32)
    for kernel_index in range(residual_kernel):
        hidden_gradient = hidden_gradient + jnp.pad(
            backward_pass[:, kernel_index * window_width : (kernel_index + 1) * window_width],
            (
                (
                    kernel_index * DILATION_SIZE,
                    (residual_kernel - 1 - kernel_index) * DILATION_SIZE,
                ),
                (0, 0),
            ),
        )
    waveform_gradient = jnp.where(
        inside_samples, hidden_gradient * negative_slope(waveform), 0.0
    ) + jnp.pad(gradient_value.astype(jnp.float32), ((DILATION_SIZE, DILATION_SIZE), (0, 0)))
    waveform_gradient = waveform_gradient.astype(jnp.bfloat16)
    d_upper = jnp.pad(waveform_gradient, ((start_offset, start_offset), (0, 0))).reshape(
        frame_count + 1, UPSAMPLE_FACTOR, window_width
    )
    zero_row = jnp.zeros((1, UPSAMPLE_FACTOR, window_width), jnp.bfloat16)
    d_taps = jnp.concatenate(
        [
            jnp.concatenate([zero_row, d_upper], axis=0),
            jnp.concatenate([d_upper, zero_row], axis=0),
        ],
        axis=1,
    )
    d_act = ups_backward(d_taps.reshape(frame_count + 2, 2 * UPSAMPLE_FACTOR * window_width))
    d_pre = jnp.where(inside_f, d_act * negative_slope(pre), 0.0).astype(jnp.bfloat16)
    g_wpre = contract_rows(patches, d_pre)
    g_bpre = jnp.sum(d_pre.astype(jnp.float32), axis=0)
    return (output_rows, (g_wpre, g_bpre, g_wres, g_bres))


def on_device(
    src_mel, owner, dst_pos, keep, cotangent, w_pre, b_pre, w_ups, upsample_bias, w_res, b_res
):
    owners_count = lax.axis_size("dp")
    seg_rows = src_mel[0]
    seg_count = seg_rows.shape[0]
    mel_bins = w_pre.shape[0] // KPRE
    pick = jnp.arange(owners_count, dtype=jnp.int32)[:, None] == owner[0][None, :]
    seg_width = seg_rows.shape[1]
    header = jnp.stack([dst_pos[0] + 1, keep[0]], axis=1).astype(jnp.bfloat16)
    seg_ext = jnp.concatenate([seg_rows, header], axis=1)
    outgoing = jnp.dot(
        pick.astype(jnp.bfloat16), seg_ext, preferred_element_type=jnp.float32
    ).astype(jnp.bfloat16)
    arrived = lax.all_to_all(outgoing, "dp", split_axis=0, concat_axis=0, tiled=True)
    slot_code = arrived[:, seg_width].astype(jnp.int32)
    keep_code = arrived[:, seg_width + 1].astype(jnp.int32)
    place = (slot_code - 1)[:, None] == jnp.arange(seg_count, dtype=jnp.int32)[None, :]
    mel_segs = contract_rows(place.astype(jnp.bfloat16), arrived[:, :seg_width]).astype(
        jnp.bfloat16
    )
    keep_segs = jnp.sum(jnp.where(place, keep_code[:, None], 0), axis=0)
    mel = mel_segs.reshape(seg_count * (mel_segs.shape[1] // mel_bins), mel_bins)
    frame_count = mel.shape[0]
    mel_ext = with_halo(mel, (("tm", 0),), KPRE // 2 + 1)
    first_frame0 = lax.axis_index("tm") * frame_count
    total = lax.axis_size("tm") * frame_count
    cot = cotangent[0]
    marks = jnp.repeat(keep_segs, cot.shape[0] // seg_count)
    gradient_value = jnp.where(marks[:, None] > 0, cot, jnp.zeros_like(cot))
    whole = lax.all_gather(w_ups, "tm", axis=0, tiled=True)

    def ups_forward(act):
        return jnp.dot(act, whole, preferred_element_type=jnp.float32)

    def ups_backward(d_taps):
        return contract_cols(d_taps, whole)

    output_rows, grads = local_pass(
        mel_ext,
        gradient_value,
        first_frame0,
        total,
        w_pre,
        b_pre,
        ups_forward,
        ups_backward,
        upsample_bias,
        w_res,
        b_res,
    )
    summed = lax.psum(grads, ("dp", "tm"))
    return (output_rows[None], summed[0], summed[1], summed[2], summed[3])


def solution(mesh):
    in_specs = (
        P("tm", "dp", None),
        P("tm", "dp"),
        P("tm", "dp"),
        P("tm", "dp"),
        P("dp", "tm", None),
        P(),
        P(),
        P("tm", None),
        P(),
        P(),
        P(),
    )
    out_specs = (P("dp", "tm", None), P(), P(), P(), P())
    return jax.shard_map(
        on_device, mesh=mesh, in_specs=in_specs, out_specs=out_specs, check_vma=False
    )
```

profile of v0, /device:TPU:0, one launch (start us, length us, event | category | flops | bytes accessed | tf_op | source)
XLA Modules:
  0.0 224.1 jit_solution(13383541488804429791)
XLA Ops:
  7.2 0.0 copy-start
  7.2 0.0 copy-start.15
  7.2 0.0 copy-start.16
  7.2 0.0 copy-start.13
  7.2 0.0 copy-start.10
  7.2 0.0 copy-start.2
  7.2 0.0 copy-start.8
  7.2 0.0 all-gather.2.cloned.1.call-start
  7.3 0.7 all-gather.2.cloned.1.call-update
  8.0 0.1 copy.26
  8.1 0.1 copy.27
  8.2 0.0 copy-done.13
  8.2 0.2 fusion.5
  8.4 0.5 broadcast.94
  8.9 0.7 reduce.4
  9.6 0.7 reshape.74
  10.3 7.4 %all-to-all-start = ((bf16[16,2,321]{2,1,0:T(2,128)(2,1)}), bf16[16,2,321]{2,1,0:T(2,128)(2,1)S(1)}, u32[]{:S(2)}, u32[]{:S(2)}) async-start(bf16[16,2,321]{2,1,0:T(2,128)(2,1)} %reshape.74), calls=%async_computation | async-start | bytes 49152 | tf_op jit(solution)/shard_map/all_to_all | solution.py:147
  17.6 0.0 all-reduce.11.cloned.1.call-start
  17.7 6.5 %all-to-all-done = bf16[16,2,321]{2,1,0:T(2,128)(2,1)S(1)} async-done(((bf16[16,2,321]{2,1,0:T(2,128)(2,1)}), bf16[16,2,321]{2,1,0:T(2,128)(2,1)S(1)}, u32[]{:S(2)}, u32[]{:S(2)}) %all-to-all-start) | async-done | bytes 20576 | tf_op jit(solution)/shard_map/all_to_all | solution.py:147
  24.2 0.1 reshape.75
  24.3 0.2 convert_reduce_fusion.2
  24.5 0.1 convolution_convert_fusion.1
  24.6 0.1 reshape.66
  24.7 1.3 collective-permute-start.1
  26.0 0.1 select_reduce_fusion
  26.2 0.1 broadcast_in_dim.91
  26.2 0.1 gt.27
  26.3 0.1 fusion.42
  26.5 0.4 fusion.43
  26.9 0.0 copy-start.11
  26.9 0.1 fusion.44
  27.1 4.5 %collective-permute-start = (bf16[4,80]{1,0:T(4,128)(2,1)S(1)}, bf16[4,80]{1,0:T(4,128)(2,1)S(1)}, u32[]{:S(2)}, u32[]{:S(2)}) collective-permute-start(bf16[4,80]{1,0:T(4,128)(2,1)S(1)} %get-tuple-element.27), channel_id=1, source_target_pairs={{0,1},{2,3},{4,5},{6,7},{8,9},{10,11},{12,13},{14,15},{16,17},{18,... | collective-permute-start | bytes 1928 | tf_op jit(solution)/shard_map/ppermute | solution.py:16
  31.6 0.0 collective-permute-done.1
  31.6 1.3 collective-permute-done
  33.0 0.1 concatenate.36
  33.1 0.0 copy-start.5
  33.1 0.2 convolution_add_fusion.1
  33.4 0.0 copy-start.3
  33.4 35.7 %all-gather.2.cloned.1.call-done = bf16[512,4096]{1,0:T(8,128)(2,1)} async-done(((bf16[256,4096]{1,0:T(8,128)(2,1)}), bf16[512,4096]{1,0:T(8,128)(2,1)}) %all-gather.2.cloned.1.call-update) | async-done | bytes 4194320 | tf_op jit(solution)/shard_map/all_gather | solution.py:163
  69.1 3.1 %fusion.19 = f32[66,4096]{1,0:T(8,128)S(1)} fusion(bf16[512,4096]{1,0:T(8,128)(2,1)} %all-gather.2.cloned.1.call-done, f32[66,512]{1,0:T(8,128)S(1)} %convolution_add_fusion.1, pred[66]{0:T(512)(128)(4,1)S(1)} %compare_and_fusion), kind=kOutput, calls=%fused_computation.37 | convolution fusion | flops 276993024 | bytes 5410882 | tf_op jit(solution)/shard_map/dot_general | solution.py:166
  72.2 0.0 copy-done.3
  72.2 0.4 copy.30
  72.6 0.0 copy-start.12
  72.6 0.1 slice.116
  72.7 0.1 fusion.15
  72.8 0.5 copy-done.12
  73.3 0.3 fusion.12
  73.6 0.1 fusion.14
  73.8 0.1 fusion.45
  73.9 0.1 pad_bitcast_fusion
  74.0 0.0 copy-start.4
  74.1 0.2 copy.31
  74.3 1.7 copy-done.1
  75.9 0.0 copy-done.4
  76.0 1.4 convert_reduce_fusion
  77.4 1.3 fusion.48
  78.7 1.4 fusion.16
  80.1 0.0 all-reduce.11.cloned.1.call-update
  80.2 0.2 convert_reduce_fusion.1
  80.3 39.7 %all-reduce.7 = (f32[512]{0:T(512)}, f32[256]{0:T(256)}) all-reduce(f32[512]{0:T(512)S(1)} %get-tuple-element.28, f32[256]{0:T(256)S(1)} %convert_reduce_fusion.1), channel_id=1, replica_groups=mesh['dp'=16,'tm'=2] {'dp','tm'}, use_global_device_ids=true, to_apply=%region_3.4 | all-reduce | flops 768 | bytes 6144 | tf_op jit(solution)/shard_map/psum | solution.py:184
  120.0 1.1 fusion.2
  121.1 92.8 %all-reduce.11.cloned.1.call-done = (f32[560,512]{1,0:T(8,128)}, f32[768,256]{1,0:T(8,128)}) async-done(((f32[560,512]{1,0:T(8,128)}, f32[768,256]{1,0:T(8,128)}), (f32[560,512]{1,0:T(8,128)}, f32[768,256]{1,0:T(8,128)})) %all-reduce.11.cloned.1.call-update) | async-done | bytes 1933328 | tf_op jit(solution)/shard_map/psum | solution.py:184
  213.9 2.4 %copy.38 = f32[560,512]{1,0:T(8,128)} copy(f32[560,512]{1,0:T(8,128)} %get-tuple-element.31) | data formatting | bytes 2293760
  216.3 0.9 copy.39
  (30 shorter events, 0.2 us)
Async XLA Ops:
  7.2 25.9 %copy-start = (bf16[560,512]{1,0:T(8,128)(2,1)S(1)}, bf16[560,512]{1,0:T(8,128)(2,1)}, u32[]{:S(2)}) copy-start(bf16[560,512]{1,0:T(8,128)(2,1)} %param.16) | copy-start | bytes 1720324
  7.2 0.8 copy-start.15
  7.2 0.9 copy-start.16
  7.2 1.0 copy-start.13
  7.2 1.0 copy-start.10
  7.2 19.1 %copy-start.2 = (bf16[1,512,256]{2,1,0:T(8,128)(2,1)S(1)}, bf16[1,512,256]{2,1,0:T(8,128)(2,1)}, u32[]{:S(2)}) copy-start(bf16[1,512,256]{2,1,0:T(8,128)(2,1)} %param.15) | copy-start | bytes 786436
  7.2 19.3 %copy-start.8 = (bf16[768,256]{1,0:T(8,128)(2,1)S(1)}, bf16[768,256]{1,0:T(8,128)(2,1)}, u32[]{:S(2)}) copy-start(bf16[768,256]{1,0:T(8,128)(2,1)} %param.20) | copy-start | bytes 1179652
  7.2 61.9 %all-gather.2.cloned.1.call-start = ((), (), s32[]{:S(2)}) async-start(), calls=%async_computation.1 | async-start | bytes 6291456 | tf_op jit(solution)/shard_map/all_gather | solution.py:163
  10.3 13.9 %all-to-all-start = ((bf16[16,2,321]{2,1,0:T(2,128)(2,1)}), bf16[16,2,321]{2,1,0:T(2,128)(2,1)S(1)}, u32[]{:S(2)}, u32[]{:S(2)}) async-start(bf16[16,2,321]{2,1,0:T(2,128)(2,1)} %reshape.74), calls=%async_computation | async-start | bytes 49152 | tf_op jit(solution)/shard_map/all_to_all | solution.py:147
  17.6 196.3 %all-reduce.11.cloned.1.call-start = ((), (), s32[]{:S(2)}) async-start(), calls=%async_computation.2 | async-start | bytes 3866624 | tf_op jit(solution)/shard_map/psum | solution.py:184
  24.7 6.9 %collective-permute-start.1 = (bf16[4,80]{1,0:T(4,128)(2,1)S(1)}, bf16[4,80]{1,0:T(4,128)(2,1)S(1)}, u32[]{:S(2)}, u32[]{:S(2)}) collective-permute-start(bf16[4,80]{1,0:T(4,128)(2,1)S(1)} %get-tuple-element.26), channel_id=1, source_target_pairs={{1,0},{3,2},{5,4},{7,6},{9,8},{11,10},{13,12},{15,14},{17,16},{19,... | collective-permute-start | bytes 1928 | tf_op jit(solution)/shard_map/ppermute | solution.py:19
  26.9 6.2 %copy-start.11 = (f32[512]{0:T(512)S(1)}, f32[512]{0:T(512)}, u32[]{:S(2)}) copy-start(f32[512]{0:T(512)} %param.17) | copy-start | bytes 6148
  27.1 5.8 %collective-permute-start = (bf16[4,80]{1,0:T(4,128)(2,1)S(1)}, bf16[4,80]{1,0:T(4,128)(2,1)S(1)}, u32[]{:S(2)}, u32[]{:S(2)}) collective-permute-start(bf16[4,80]{1,0:T(4,128)(2,1)S(1)} %get-tuple-element.27), channel_id=1, source_target_pairs={{0,1},{2,3},{4,5},{6,7},{8,9},{10,11},{12,13},{14,15},{16,17},{18,... | collective-permute-start | bytes 1928 | tf_op jit(solution)/shard_map/ppermute | solution.py:16
  33.1 39.1 %copy-start.5 = (bf16[66,560]{1,0:T(8,128)(2,1)}, bf16[66,560]{1,0:T(8,128)(2,1)S(1)}, u32[]{:S(2)}) copy-start(bf16[66,560]{1,0:T(8,128)(2,1)S(1)} %concatenate.36) | copy-start | bytes 221764
  33.4 38.8 %copy-start.3 = (f32[66,512]{1,0:T(8,128)}, f32[66,512]{1,0:T(8,128)S(1)}, u32[]{:S(2)}) copy-start(f32[66,512]{1,0:T(8,128)S(1)} %convolution_add_fusion.1) | copy-start | bytes 405508
  72.6 0.7 copy-start.12
  73.8 2.2 copy-start.1
  74.0 2.0 copy-start.4
  76.0 1.4 copy-start.6
  80.1 39.9 %copy-start.9 = (bf16[768,256]{1,0:T(8,128)(2,1)S(1)}, bf16[768,256]{1,0:T(8,128)(2,1)}, u32[]{:S(2)}) copy-start(bf16[768,256]{1,0:T(8,128)(2,1)} %param.20) | copy-start | bytes 1179652
  80.1 39.9 %copy-start.14 = (f32[256]{0:T(256)S(1)}, f32[256]{0:T(256)}, u32[]{:S(2)}) copy-start(f32[256]{0:T(256)} %param.21) | copy-start | bytes 3076
  213.9 2.4 %copy-start.7 = (f32[768,256]{1,0:T(8,128)S(1)}, f32[768,256]{1,0:T(8,128)}, u32[]{:S(2)}) copy-start(f32[768,256]{1,0:T(8,128)} %get-tuple-element.33) | copy-start | bytes 2359300
Sparse Core Ops, SparseCore 0:
  9.6 59.4 all-gather.1
  80.3 133.6 all-reduce.10
where the time goes:
time: 224 us
  waiting for transfers between devices  137 us (61%)
  blocking collectives  39.7 us (18%)
  between operations  14.4 us (6%)
  starting transfers between devices  13.3 us (6%)
  matrix products  9.26 us (4%)
  local copies, waits for them, and re-layouts  8.51 us (4%)
    psum x1, waiting for transfers between devices, on_device(): summed = lax.psum(grads, ('dp', 'tm'))  92.8 us
    psum x1, blocking collectives, on_device(): summed = lax.psum(grads, ('dp', 'tm'))  39.7 us
    all_gather x1, waiting for transfers between devices, on_device(): whole = lax.all_gather(w_ups, 'tm', axis=0, tiled=True)  35.7 us
    all_to_all x1, starting transfers between devices, on_device(): lax.all_to_all(outgoing, 'dp', split_axis=0, concat_axis=0, tiled=True)  7.36 us
    unnamed x43, local copies, waits for them, and re-layouts  7 us
    all_to_all x1, waiting for transfers between devices, on_device(): lax.all_to_all(outgoing, 'dp', split_axis=0, concat_axis=0, tiled=True)  6.48 us
    ppermute x1, starting transfers between devices, with_halo(): lax.ppermute(lax.slice_in_dim(block, block.shape[dim] - width, None, axis...  4.54 us
  transfers between devices with their start and end apart: 5, of which 4 were waited for; matrix products, arithmetic and copies ran while one was open for 2% of the time, Pallas kernels for 0%

commit v1 on v0

--- a/solution.py
+++ b/solution.py
@@ -181,7 +181,7 @@
         w_res,
         b_res,
     )
-    summed = lax.psum(grads, ("dp", "tm"))
+    summed = lax.psum(lax.psum(grads, "tm"), "dp")
     return (output_rows[None], summed[0], summed[1], summed[2], summed[3])
 
 

time: 224 us -> 251 us (1.12)
  waiting for transfers between devices: 137 us -> 165 us
    psum x1 -> x2, waiting for transfers between devices: 92.8 us -> 121 us  [on_device(): summed = lax.psum(lax.psum(grads, 'tm'), 'dp')]
    psum x1 -> x2, blocking collectives: 39.7 us -> 38.2 us  [on_device(): summed = lax.psum(lax.psum(grads, 'tm'), 'dp')]
  transfers between devices with their start and end apart: 5 -> 6, of which waited for: 4 -> 5; matrix products, arithmetic and copies ran while one was open for 2% -> 2% of each run, Pallas kernels for 0% -> 0%
where the time goes in v1:
time: 251 us; the launch traced here: 250 us
  waiting for transfers between devices  165 us (66%)
  blocking collectives  38.2 us (15%)
  between operations  14.2 us (6%)
  starting transfers between devices  13.3 us (5%)
  matrix products  9.26 us (4%)
  local copies, waits for them, and re-layouts  8.47 us (3%)
    psum x2, waiting for transfers between devices, on_device(): summed = lax.psum(lax.psum(grads, 'tm'), 'dp')  121 us
    psum x2, blocking collectives, on_device(): summed = lax.psum(lax.psum(grads, 'tm'), 'dp')  38.2 us
    all_gather x1, waiting for transfers between devices, on_device(): whole = lax.all_gather(w_ups, 'tm', axis=0, tiled=True)  35.7 us
    all_to_all x1, starting transfers between devices, on_device(): lax.all_to_all(outgoing, 'dp', split_axis=0, concat_axis=0, tiled=True)  7.36 us
    unnamed x43, local copies, waits for them, and re-layouts  6.96 us
    all_to_all x1, waiting for transfers between devices, on_device(): lax.all_to_all(outgoing, 'dp', split_axis=0, concat_axis=0, tiled=True)  6.48 us
  transfers between devices with their start and end apart: 6, of which 5 were waited for; matrix products, arithmetic and copies ran while one was open for 2% of the time, Pallas kernels for 0%

profile of v1, /device:TPU:0, one launch (start us, length us, event | category | flops | bytes accessed | tf_op | source)
XLA Modules:
  0.0 250.5 jit_solution(7799366341063224146)
XLA Ops:
  7.2 0.0 copy-start
  7.2 0.0 copy-start.15
  7.2 0.0 copy-start.16
  7.2 0.0 copy-start.8
  7.2 0.0 all-gather.2.cloned.1.call-start
  7.3 0.7 all-gather.2.cloned.1.call-update
  8.0 0.1 copy.26
  8.1 0.1 copy.27
  8.2 0.2 fusion.5
  8.4 0.5 broadcast.94
  8.9 0.7 reduce.4
  9.6 0.7 reshape.74
  10.3 7.4 %all-to-all-start = ((bf16[16,2,321]{2,1,0:T(2,128)(2,1)}), bf16[16,2,321]{2,1,0:T(2,128)(2,1)S(1)}, u32[]{:S(2)}, u32[]{:S(2)}) async-start(bf16[16,2,321]{2,1,0:T(2,128)(2,1)} %reshape.74), calls=%async_computation | async-start | bytes 49152 | tf_op jit(solution)/shard_map/all_to_all | solution.py:147
  17.6 0.0 all-reduce.16.cloned.1.call-start
  17.7 6.5 %all-to-all-done = bf16[16,2,321]{2,1,0:T(2,128)(2,1)S(1)} async-done(((bf16[16,2,321]{2,1,0:T(2,128)(2,1)}), bf16[16,2,321]{2,1,0:T(2,128)(2,1)S(1)}, u32[]{:S(2)}, u32[]{:S(2)}) %all-to-all-start) | async-done | bytes 20576 | tf_op jit(solution)/shard_map/all_to_all | solution.py:147
  24.2 0.1 reshape.75
  24.3 0.2 convert_reduce_fusion.2
  24.5 0.1 convolution_convert_fusion.1
  24.6 0.1 reshape.66
  24.7 1.3 collective-permute-start.1
  26.0 0.1 select_reduce_fusion
  26.2 0.1 broadcast_in_dim.91
  26.2 0.1 gt.27
  26.3 0.1 fusion.42
  26.5 0.4 fusion.43
  26.9 0.0 copy-start.11
  26.9 0.1 fusion.44
  27.1 4.5 %collective-permute-start = (bf16[4,80]{1,0:T(4,128)(2,1)S(1)}, bf16[4,80]{1,0:T(4,128)(2,1)S(1)}, u32[]{:S(2)}, u32[]{:S(2)}) collective-permute-start(bf16[4,80]{1,0:T(4,128)(2,1)S(1)} %get-tuple-element.31), channel_id=1, source_target_pairs={{0,1},{2,3},{4,5},{6,7},{8,9},{10,11},{12,13},{14,15},{16,17},{18,... | collective-permute-start | bytes 1928 | tf_op jit(solution)/shard_map/ppermute | solution.py:16
  31.6 0.0 collective-permute-done.1
  31.6 1.3 collective-permute-done
  33.0 0.1 concatenate.36
  33.1 0.0 copy-start.5
  33.1 0.2 convolution_add_fusion.1
  33.4 0.0 copy-start.3
  33.4 35.7 %all-gather.2.cloned.1.call-done = bf16[512,4096]{1,0:T(8,128)(2,1)} async-done(((bf16[256,4096]{1,0:T(8,128)(2,1)}), bf16[512,4096]{1,0:T(8,128)(2,1)}) %all-gather.2.cloned.1.call-update) | async-done | bytes 4194320 | tf_op jit(solution)/shard_map/all_gather | solution.py:163
  69.1 3.1 %fusion.19 = f32[66,4096]{1,0:T(8,128)S(1)} fusion(bf16[512,4096]{1,0:T(8,128)(2,1)} %all-gather.2.cloned.1.call-done, f32[66,512]{1,0:T(8,128)S(1)} %convolution_add_fusion.1, pred[66]{0:T(512)(128)(4,1)S(1)} %compare_and_fusion), kind=kOutput, calls=%fused_computation.37 | convolution fusion | flops 276993024 | bytes 5410882 | tf_op jit(solution)/shard_map/dot_general | solution.py:166
  72.2 0.4 copy.30
  72.6 0.0 copy-start.12
  72.6 0.1 slice.116
  72.7 0.1 fusion.15
  72.8 0.5 copy-done.12
  73.3 0.3 fusion.12
  73.6 0.1 pad_bitcast_fusion
  73.8 0.0 copy-start.4
  73.8 0.2 copy.31
  74.0 0.1 fusion.14
  74.2 0.1 fusion.45
  74.3 1.6 copy-done.1
  75.9 1.4 convert_reduce_fusion
  77.3 1.3 fusion.48
  78.7 1.4 fusion.16
  80.1 0.0 all-reduce.16.cloned.1.call-update
  80.1 0.0 copy-start.9
  80.1 0.0 copy-start.14
  80.1 0.0 all-reduce.14.cloned.1.call-start
  80.2 59.6 %all-reduce.16.cloned.1.call-done = (f32[560,512]{1,0:T(8,128)}, f32[768,256]{1,0:T(8,128)}) async-done(((f32[560,512]{1,0:T(8,128)}, f32[768,256]{1,0:T(8,128)}), (f32[560,512]{1,0:T(8,128)}, f32[768,256]{1,0:T(8,128)})) %all-reduce.16.cloned.1.call-update) | async-done | bytes 1933328 | tf_op jit(solution)/shard_map/psum | solution.py:184
  139.8 0.0 all-reduce.14.cloned.1.call-update
  139.8 0.2 convert_reduce_fusion.1
  140.0 4.9 %all-reduce.9 = (f32[512]{0:T(512)S(1)}, f32[256]{0:T(256)S(1)}) all-reduce(f32[512]{0:T(512)S(1)} %get-tuple-element.32, f32[256]{0:T(256)S(1)} %convert_reduce_fusion.1), channel_id=1, replica_groups=mesh['dp'=16,'tm'=2] {'tm'}, use_global_device_ids=true, to_apply=%region_4.5 | all-reduce | flops 768 | bytes 6144 | tf_op jit(solution)/shard_map/psum | solution.py:184
  144.9 33.3 %all-reduce.7 = (f32[512]{0:T(512)}, f32[256]{0:T(256)}) all-reduce(f32[512]{0:T(512)S(1)} %get-tuple-element.11, f32[256]{0:T(256)S(1)} %get-tuple-element.12), channel_id=1, replica_groups=mesh['dp'=16,'tm'=2] {'dp'}, use_global_device_ids=true, to_apply=%region_5.6 | all-reduce | flops 768 | bytes 6144 | tf_op jit(solution)/shard_map/psum | solution.py:184
  178.2 1.1 fusion.2
  179.3 61.4 %all-reduce.14.cloned.1.call-done = (f32[560,512]{1,0:T(8,128)}, f32[768,256]{1,0:T(8,128)}) async-done(((f32[560,512]{1,0:T(8,128)}, f32[768,256]{1,0:T(8,128)}), (f32[560,512]{1,0:T(8,128)}, f32[768,256]{1,0:T(8,128)})) %all-reduce.14.cloned.1.call-update) | async-done | bytes 1933328 | tf_op jit(solution)/shard_map/psum | solution.py:184
  240.6 2.4 copy.40
  243.0 0.9 copy.41
  (34 shorter events, 0.2 us)
Async XLA Ops:
  7.2 25.9 %copy-start = (bf16[560,512]{1,0:T(8,128)(2,1)S(1)}, bf16[560,512]{1,0:T(8,128)(2,1)}, u32[]{:S(2)}) copy-start(bf16[560,512]{1,0:T(8,128)(2,1)} %param.16) | copy-start | bytes 1720324
  7.2 0.8 copy-start.15
  7.2 0.9 copy-start.16
  7.2 1.0 copy-start.13
  7.2 1.0 copy-start.10
  7.2 19.1 %copy-start.2 = (bf16[1,512,256]{2,1,0:T(8,128)(2,1)S(1)}, bf16[1,512,256]{2,1,0:T(8,128)(2,1)}, u32[]{:S(2)}) copy-start(bf16[1,512,256]{2,1,0:T(8,128)(2,1)} %param.15) | copy-start | bytes 786436
  7.2 19.3 %copy-start.8 = (bf16[768,256]{1,0:T(8,128)(2,1)S(1)}, bf16[768,256]{1,0:T(8,128)(2,1)}, u32[]{:S(2)}) copy-start(bf16[768,256]{1,0:T(8,128)(2,1)} %param.20) | copy-start | bytes 1179652
  7.2 61.9 %all-gather.2.cloned.1.call-start = ((), (), s32[]{:S(2)}) async-start(), calls=%async_computation.1 | async-start | bytes 6291456 | tf_op jit(solution)/shard_map/all_gather | solution.py:163
  10.3 13.9 %all-to-all-start = ((bf16[16,2,321]{2,1,0:T(2,128)(2,1)}), bf16[16,2,321]{2,1,0:T(2,128)(2,1)S(1)}, u32[]{:S(2)}, u32[]{:S(2)}) async-start(bf16[16,2,321]{2,1,0:T(2,128)(2,1)} %reshape.74), calls=%async_computation | async-start | bytes 49152 | tf_op jit(solution)/shard_map/all_to_all | solution.py:147
  17.6 122.1 %all-reduce.16.cloned.1.call-start = ((), (), s32[]{:S(2)}) async-start(), calls=%async_computation.3 | async-start | bytes 3866624 | tf_op jit(solution)/shard_map/psum | solution.py:184
  24.7 6.9 %collective-permute-start.1 = (bf16[4,80]{1,0:T(4,128)(2,1)S(1)}, bf16[4,80]{1,0:T(4,128)(2,1)S(1)}, u32[]{:S(2)}, u32[]{:S(2)}) collective-permute-start(bf16[4,80]{1,0:T(4,128)(2,1)S(1)} %get-tuple-element.30), channel_id=1, source_target_pairs={{1,0},{3,2},{5,4},{7,6},{9,8},{11,10},{13,12},{15,14},{17,16},{19,... | collective-permute-start | bytes 1928 | tf_op jit(solution)/shard_map/ppermute | solution.py:19
  26.9 6.2 %copy-start.11 = (f32[512]{0:T(512)S(1)}, f32[512]{0:T(512)}, u32[]{:S(2)}) copy-start(f32[512]{0:T(512)} %param.17) | copy-start | bytes 6148
  27.1 5.8 %collective-permute-start = (bf16[4,80]{1,0:T(4,128)(2,1)S(1)}, bf16[4,80]{1,0:T(4,128)(2,1)S(1)}, u32[]{:S(2)}, u32[]{:S(2)}) collective-permute-start(bf16[4,80]{1,0:T(4,128)(2,1)S(1)} %get-tuple-element.31), channel_id=1, source_target_pairs={{0,1},{2,3},{4,5},{6,7},{8,9},{10,11},{12,13},{14,15},{16,17},{18,... | collective-permute-start | bytes 1928 | tf_op jit(solution)/shard_map/ppermute | solution.py:16
  33.1 39.1 %copy-start.5 = (bf16[66,560]{1,0:T(8,128)(2,1)}, bf16[66,560]{1,0:T(8,128)(2,1)S(1)}, u32[]{:S(2)}) copy-start(bf16[66,560]{1,0:T(8,128)(2,1)S(1)} %concatenate.36) | copy-start | bytes 221764
  33.4 38.8 %copy-start.3 = (f32[66,512]{1,0:T(8,128)}, f32[66,512]{1,0:T(8,128)S(1)}, u32[]{:S(2)}) copy-start(f32[66,512]{1,0:T(8,128)S(1)} %convolution_add_fusion.1) | copy-start | bytes 405508
  72.6 0.7 copy-start.12
  73.7 2.2 copy-start.1
  73.8 2.1 copy-start.4
  75.9 1.4 copy-start.6
  80.1 98.1 %copy-start.9 = (bf16[768,256]{1,0:T(8,128)(2,1)S(1)}, bf16[768,256]{1,0:T(8,128)(2,1)}, u32[]{:S(2)}) copy-start(bf16[768,256]{1,0:T(8,128)(2,1)} %param.20) | copy-start | bytes 1179652
  80.1 98.1 %copy-start.14 = (f32[256]{0:T(256)S(1)}, f32[256]{0:T(256)}, u32[]{:S(2)}) copy-start(f32[256]{0:T(256)} %param.21) | copy-start | bytes 3076
  80.1 160.5 %all-reduce.14.cloned.1.call-start = ((), (), s32[]{:S(2)}) async-start(), calls=%async_computation.2 | async-start | bytes 3866624 | tf_op jit(solution)/shard_map/psum | solution.py:184
  240.6 2.4 copy-start.7
Sparse Core Ops, SparseCore 0:
  9.6 59.4 all-gather.1
  80.2 59.5 all-reduce.15
  143.4 97.2 all-reduce.13
